TPU v7x, 32 devices: a whole 2x2x4 slice. The times are simulated.
32 devices in a mesh: group: 4 (over z), member: 8 (over y, x, core).
Axes of the slice: x: 2, y: 2, z: 4, core: 2. Of those that a mesh axis runs over, the one named last changes fastest.
Arguments:
- query_feat: bfloat16 [4096, 4096], P(('group', 'member'))
- code_feat: bfloat16 [4096, 4096], P(('group', 'member'))
- projection: bfloat16 [4096, 1024], replicated
- hard_ids: int32 [32, 16], P(('group', 'member')), may hold values from 0 to 63, as said below
- loss_weight: float32 [4096], P(('group', 'member')), may hold values from 1 to 4
Outputs:
- query_grad: bfloat16 [4096, 4096], P(('group', 'member'))
- code_grad: bfloat16 [4096, 4096], P(('group', 'member'))
- projection_grad: float32 [4096, 1024], P(('group', 'member'))
Inputs may be any that keep to these rules, and one draw needn't show every extreme that they name: `hard_ids`: entry (owner device g * 8 + m) * 2 + slot names code rows of that device. A row names 16 different blocks, none of its own group; at most 8 of them lie in one group, and exactly 8 in some group of every row.
All inputs are finite; a program needn't handle non-finite values.
Results may differ from a plain program's by a relative error of at most 0.02.
Values may be sent and summed in bfloat16 or wider, within the bound.
No kernel may reach another device: no remote copies, remote signals or barrier semaphores. Data moves between devices by JAX's collectives and lax.ppermute only.
A program may use at most 128 MiB of HBM per device.

v0:
```python
import jax
import jax.numpy as jnp
from jax import lax
from jax.sharding import PartitionSpec as P

CB = 64
inverse_temp = 120.0
epsilon = 1e-06


def embed(features, projection):
    values = jnp.dot(features, projection, preferred_element_type=jnp.float32)
    inverse = lax.rsqrt(jnp.sum(values * values, axis=1) + epsilon)
    unit_vec = values * inverse[:, None]
    return (unit_vec, inverse, unit_vec.astype(jnp.bfloat16))


def norm_back(upstream, unit_vec, inverse):
    inner_prod = jnp.sum(unit_vec * upstream, axis=1, keepdims=True)
    return (inverse[:, None] * (upstream - unit_vec * inner_prod)).astype(jnp.bfloat16)


def shift_all(x, axis):
    size = lax.axis_size(axis)
    index = lax.axis_index(axis)
    got = [x]
    for s in range(1, size):
        got.append(lax.ppermute(x, axis, [(i, (i + s) % size) for i in range(size)]))
    order = (index - jnp.arange(size)) % size
    return jax.tree.map(lambda *xs: jnp.take(jnp.stack(xs, axis=0), order, axis=0), *got)


def exchange(parts, axis):
    size = lax.axis_size(axis)
    index = lax.axis_index(axis)
    got = [jnp.take(parts, index, axis=0)]
    for s in range(1, size):
        sent = jnp.take(parts, (index + s) % size, axis=0)
        got.append(lax.ppermute(sent, axis, [(i, (i + s) % size) for i in range(size)]))
    stacked = jnp.stack(got, axis=0)
    return jnp.take(stacked, (index - jnp.arange(size)) % size, axis=0)


def body(query_feat, code_feat, projection, hard_ids, loss_weight):
    groups = lax.axis_size("group")
    members = lax.axis_size("member")
    group_index = lax.axis_index("group")
    member_index = lax.axis_index("member")
    queries_dev = query_feat.shape[0]
    feat_width = query_feat.shape[1]
    emb_width = projection.shape[1]
    slot_count = queries_dev // CB
    per_group = members * slot_count
    group_span = members * queries_dev
    rows_dev = feat_width // (groups * members)
    feats = jnp.stack([query_feat, code_feat], axis=0).reshape(
        2, queries_dev, groups, members, rows_dev
    )
    feats = jnp.transpose(feats, (3, 0, 1, 2, 4))
    feat_cols = lax.all_to_all(feats, "member", split_axis=0, concat_axis=0, tiled=True)
    q_unit, q_inv, q_emb = embed(query_feat, projection)
    code_values = lax.all_gather(
        jnp.dot(code_feat, projection, preferred_element_type=jnp.float32),
        "member",
        axis=0,
        tiled=True,
    )
    c_inv = lax.rsqrt(jnp.sum(code_values * code_values, axis=1) + epsilon)
    c_unit = code_values * c_inv[:, None]
    group_codes = c_unit.astype(jnp.bfloat16)
    q_all = lax.all_to_all(
        jnp.broadcast_to(q_emb[None], (groups, queries_dev, emb_width)),
        "group",
        split_axis=0,
        concat_axis=0,
        tiled=True,
    )
    ids_all = shift_all(hard_ids[0], "group")
    block_ids = group_index * per_group + jnp.arange(per_group, dtype=jnp.int32)
    asked = jnp.any(ids_all[:, :, None] == block_ids[None, None, :], axis=1)
    own = jnp.arange(groups, dtype=jnp.int32) == group_index
    block_mask = asked | own[:, None]
    col_mask = jnp.broadcast_to(block_mask[:, :, None], (groups, per_group, CB)).reshape(
        groups, 1, group_span
    )
    scores = inverse_temp * jnp.einsum(
        "gqe,ke->gqk", q_all, group_codes, preferred_element_type=jnp.float32
    )
    scores = jnp.where(col_mask, scores, -jnp.inf)
    part_max = jnp.max(scores, axis=2)
    safe_max = jnp.where(part_max > -jnp.inf, part_max, 0.0)
    part_sum = jnp.sum(jnp.exp(scores - safe_max[:, :, None]), axis=2)
    weights_row = jnp.broadcast_to(loss_weight[None], (groups, queries_dev))
    stats = shift_all(jnp.stack([part_max, part_sum, weights_row], axis=0), "group")
    w_all = stats[:, 2, 0]
    row_max = jnp.max(stats[:, 0], axis=0)
    row_sum = jnp.sum(stats[:, 1] * jnp.exp(stats[:, 0] - row_max[None]), axis=0)
    log_total = row_max + jnp.log(row_sum)
    offsets = jnp.arange(queries_dev, dtype=jnp.int32)
    columns = jnp.arange(group_span, dtype=jnp.int32)
    positive = (columns[None, :] == (member_index * queries_dev + offsets)[:, None]).astype(
        jnp.float32
    )
    positive = positive[None] * own[:, None, None].astype(jnp.float32)
    factor = w_all * inverse_temp
    grad = (factor[:, :, None] * (jnp.exp(scores - log_total[:, :, None]) - positive)).astype(
        jnp.bfloat16
    )
    code_terms = None
    for g in range(groups):
        term = jnp.dot(grad[g].T, q_all[g], preferred_element_type=jnp.float32)
        term = jnp.where(g == group_index, term, term.astype(jnp.bfloat16).astype(jnp.float32))
        code_terms = term if code_terms is None else code_terms + term
    code_sum = code_terms.astype(jnp.bfloat16)
    grad_dq, code_sum = lax.optimization_barrier((grad, code_sum))
    code_delta = lax.psum(code_sum, "member").astype(jnp.float32)
    delta_parts = jnp.einsum(
        "gqk,ke->gqe", grad_dq, group_codes, preferred_element_type=jnp.float32
    )
    returned = exchange(delta_parts.astype(jnp.bfloat16), "group").astype(jnp.float32)
    own_part = jnp.take(delta_parts, group_index, axis=0)
    query_delta = own_part + jnp.sum(jnp.where(own[:, None, None], 0.0, returned), axis=0)
    dz_query = norm_back(query_delta, q_unit, q_inv)
    dz_code_all = norm_back(code_delta, c_unit, c_inv)
    dz_code = lax.dynamic_slice_in_dim(dz_code_all, member_index * queries_dev, queries_dev, 0)
    query_grad = jnp.einsum(
        "qe,de->qd", dz_query, projection, preferred_element_type=jnp.float32
    ).astype(jnp.bfloat16)
    code_grad = jnp.einsum(
        "qe,de->qd", dz_code, projection, preferred_element_type=jnp.float32
    ).astype(jnp.bfloat16)
    dzq_all = lax.all_to_all(
        jnp.broadcast_to(dz_query[None], (members, queries_dev, emb_width)),
        "member",
        split_axis=0,
        concat_axis=0,
        tiled=True,
    )
    dzc_all = dz_code_all.reshape(members, queries_dev, emb_width)
    proj_parts = jnp.einsum(
        "mqgr,mqe->gre", feat_cols[:, 0], dzq_all, preferred_element_type=jnp.float32
    ) + jnp.einsum("mqgr,mqe->gre", feat_cols[:, 1], dzc_all, preferred_element_type=jnp.float32)
    own_proj = jnp.take(proj_parts, group_index, axis=0)
    sent_proj = jnp.where(own[:, None, None], 0.0, proj_parts).astype(jnp.bfloat16)
    projection_grad = own_proj + lax.psum_scatter(
        sent_proj, "group", scatter_dimension=0, tiled=True
    ).reshape(rows_dev, emb_width).astype(jnp.float32)
    return (query_grad, code_grad, projection_grad)


def solution(mesh):
    return jax.shard_map(
        body,
        mesh=mesh,
        in_specs=(
            P(("group", "member"), None),
            P(("group", "member"), None),
            P(),
            P(("group", "member"), None),
            P(("group", "member")),
        ),
        out_specs=(
            P(("group", "member"), None),
            P(("group", "member"), None),
            P(("group", "member"), None),
        ),
        check_vma=False,
    )
```

profile of v0, /device:TPU:0, one launch (start us, length us, event | category | flops | bytes accessed | tf_op | source)
XLA Modules:
  0.0 204.6 jit_solution(2245639925189366476)
XLA Ops:
  7.2 5.8 %fusion.26 = f32[128,1024]{1,0:T(8,128)} fusion(bf16[128,4096]{1,0:T(8,128)(2,1)} %param.10, bf16[4096,1024]{1,0:T(8,128)(2,1)} %param.11), kind=kOutput, calls=%fused_computation.91 | convolution fusion | flops 1073741824 | bytes 9961472 | tf_op jit(solution)/shard_map/dot_general | solution.py:63
  13.1 3.1 %collective-permute-start = (s32[16]{0:T(128)S(1)}, s32[16]{0:T(128)S(1)}, u32[]{:S(2)}, u32[]{:S(2)}) collective-permute-start(s32[16]{0:T(128)S(1)} %bitcast.128), channel_id=1, source_target_pairs={{0,8},{8,16},{16,24},{24,0},{1,9},{9,17},{17,25},{25,1},{2,10},{10... | collective-permute-start | bytes 200 | tf_op jit(solution)/shard_map/ppermute | solution.py:28
  16.2 2.6 %collective-permute-start.1 = (s32[16]{0:T(128)S(1)}, s32[16]{0:T(128)S(1)}, u32[]{:S(2)}, u32[]{:S(2)}) collective-permute-start(s32[16]{0:T(128)S(1)} %bitcast.129), channel_id=1, source_target_pairs={{0,16},{8,24},{16,0},{24,8},{1,17},{9,25},{17,1},{25,9},{2,18},{10... | collective-permute-start | bytes 200 | tf_op jit(solution)/shard_map/ppermute | solution.py:28
  18.8 1.4 collective-permute-start.2
  20.2 5.0 %multiply_reduce_fusion.2 = (f32[128]{0:T(128)S(1)}, f32[128,1024]{1,0:T(8,128)S(1)}) fusion(bf16[128,4096]{1,0:T(8,128)(2,1)S(1)} %copy-done.5, bf16[4096,1024]{1,0:T(8,128)(2,1)} %param.11), kind=kOutput, calls=%fused_computation.31 | convolution fusion | flops 1074003840 | bytes 9961984 | tf_op jit(solution)/shard_map/dot_general | solution.py:12
  25.3 1.1 broadcast_in_dim.126
  26.4 3.6 %all-to-all-start = ((bf16[4,128,1024]{2,1,0:T(8,128)(2,1)}), bf16[4,128,1024]{2,1,0:T(8,128)(2,1)S(1)}, u32[]{:S(2)}, u32[]{:S(2)}) async-start(bf16[4,128,1024]{2,1,0:T(8,128)(2,1)} %broadcast_in_dim.126), calls=%async_computation | async-start | bytes 2097152 | tf_op jit(solution)/shard_map/all_to_all | solution.py:71
  30.1 1.3 copy.23
  31.4 1.3 copy.24
  32.8 1.4 maximum_bitcast_fusion
  34.2 0.9 fusion.6
  35.1 1.5 copy.25
  37.5 15.0 %all-gather.2.cloned.1.call-done = f32[1024,1024]{1,0:T(8,128)} async-done(((f32[128,1024]{1,0:T(8,128)}), f32[1024,1024]{1,0:T(8,128)}) %all-gather.2.cloned.1.call-update) | async-done | bytes 4194320 | tf_op jit(solution)/shard_map/all_gather | solution.py:62
  52.6 2.5 %multiply_reduce_fusion = f32[1024]{0:T(1024)S(1)} fusion(f32[1024,1024]{1,0:T(8,128)} %all-gather.2.cloned.1.call-done), kind=kLoop, calls=%fused_computation.11 | loop fusion | flops 2096128 | bytes 4198400 | tf_op jit(solution)/shard_map/reduce_sum | solution.py:68
  55.1 4.4 %all-to-all-start.1 = ((bf16[8,2,128,4,128]{2,4,3,1,0:T(8,128)(2,1)}), bf16[8,2,128,4,128]{2,4,3,1,0:T(8,128)(2,1)}, u32[]{:S(2)}, u32[]{:S(2)}) async-start(bf16[8,2,128,4,128]{2,4,3,1,0:T(8,128)(2,1)} %copy.25), calls=%async_computation.1 | async-start | bytes 4194304 | tf_op jit(solution)/shard_map/all_to_all | solution.py:60
  59.5 3.6 %fusion.24 = (f32[4,128]{1,0:T(4,128)S(1)}, f32[4,128,1024]{2,1,0:T(8,128)S(1)}) fusion(bf16[4,128,1024]{2,1,0:T(8,128)(2,1)S(1)} %all-to-all-done, f32[1024,1024]{1,0:T(8,128)} %all-gather.2.cloned.1.call-done, f32[1024]{0:T(1024)S(1)} %add_rsqrt_fusion, pred[4,1024]{1,0:T(4,128)(4,1)S(1)} %broadcast_in_dim.124), kind=kOutput, calls=%fused_computation.89 | convolution fusion | flops 1077411328 | bytes 7350272 | tf_op jit(solution)/shard_map/gqe,ke->gqk/dot_general | solution.py:86
  63.8 2.5 %collective-permute-start.4 = (f32[3,4,128]{2,1,0:T(4,128)S(1)}, f32[3,4,128]{2,1,0:T(4,128)S(1)}, u32[]{:S(2)}, u32[]{:S(2)}) collective-permute-start(f32[3,4,128]{2,1,0:T(4,128)S(1)} %get-tuple-element.38), channel_id=1, source_target_pairs={{0,16},{8,24},{16,0},{24,8},{1,17},{9,25},{17,1},{25,9},{2,18},{10... | collective-permute-start | bytes 18440 | tf_op jit(solution)/shard_map/ppermute | solution.py:28
  66.3 1.4 collective-permute-start.5
  67.7 0.6 collective-permute-start.3
  68.4 1.5 collective-permute-done.5
  69.9 3.2 %collective-permute-done.3 = f32[3,4,128]{2,1,0:T(4,128)S(1)} collective-permute-done((f32[3,4,128]{2,1,0:T(4,128)S(1)}, f32[3,4,128]{2,1,0:T(4,128)S(1)}, u32[]{:S(2)}, u32[]{:S(2)}) %collective-permute-start.3) | collective-permute-done | bytes 6176 | tf_op jit(solution)/shard_map/ppermute | solution.py:28
  73.2 0.6 gather_fusion.1
  73.9 1.6 multiply_convert_fusion.1
  75.5 0.7 fusion.11
  76.2 0.7 fusion.12
  76.9 0.7 fusion.10
  77.7 2.4 %add_convert_fusion = bf16[1024,1024]{1,0:T(8,128)(2,1)} fusion(f32[1024,1024]{1,0:T(8,128)S(1)} %fusion.10, f32[1024,1024]{1,0:T(8,128)S(1)} %fusion.11, f32[1024,1024]{1,0:T(8,128)S(1)} %fusion.12, pred[]{:T(512)S(6)} %eq.75, pred[]{:T(512)S(6)} %eq.74, pred[]{:T(512)S(6)} %eq.73, pred[]{:T(512)S(6)} %eq.72, bf16[4,128,1024]{2,1,0:T(8,128)(2,1)S(1)} %all-to-all-done, ...), kind=kOutput, calls=%fused_computation.10 | convolution fusion | flops 285212672 | bytes 15204356 | tf_op jit(solution)/shard_map/dot_general | solution.py:111
  80.1 3.8 %fusion.25 = (bf16[4,128,1024]{2,1,0:T(8,128)(2,1)S(1)}, f32[4,128,1024]{2,1,0:T(8,128)S(1)}) fusion(bf16[4,128,1024]{2,1,0:T(8,128)(2,1)} %copy-done.1, f32[1024,1024]{1,0:T(8,128)} %all-gather.2.cloned.1.call-done, f32[1024]{0:T(1024)S(1)} %add_rsqrt_fusion), kind=kOutput, calls=%fused_computation.90 | convolution fusion | flops 1076363264 | bytes 8392704 | tf_op jit(solution)/shard_map/gqk,ke->gqe/dot_general | solution.py:117
  83.9 0.9 dynamic-slice_select_fusion
  85.4 3.3 %collective-permute-start.8 = (bf16[128,1024]{1,0:T(8,128)(2,1)}, bf16[128,1024]{1,0:T(8,128)(2,1)S(1)}, u32[]{:S(2)}, u32[]{:S(2)}) collective-permute-start(bf16[128,1024]{1,0:T(8,128)(2,1)} %get-tuple-element.34), channel_id=1, source_target_pairs={{0,24},{8,0},{16,8},{24,16},{1,25},{9,1},{17,9},{25,17},{2,26},{10... | collective-permute-start | bytes 786440 | tf_op jit(solution)/shard_map/ppermute | solution.py:39
  88.7 7.4 %collective-permute-done.6 = bf16[128,1024]{1,0:T(8,128)(2,1)S(1)} collective-permute-done((bf16[128,1024]{1,0:T(8,128)(2,1)}, bf16[128,1024]{1,0:T(8,128)(2,1)S(1)}, u32[]{:S(2)}, u32[]{:S(2)}) %collective-permute-start.6) | collective-permute-done | bytes 262176 | tf_op jit(solution)/shard_map/ppermute | solution.py:39
  96.2 8.9 %collective-permute-done.7 = bf16[128,1024]{1,0:T(8,128)(2,1)S(1)} collective-permute-done((bf16[128,1024]{1,0:T(8,128)(2,1)}, bf16[128,1024]{1,0:T(8,128)(2,1)S(1)}, u32[]{:S(2)}, u32[]{:S(2)}) %collective-permute-start.7) | collective-permute-done | bytes 262176 | tf_op jit(solution)/shard_map/ppermute | solution.py:39
  105.1 1.1 pad_maximum_fusion
  106.2 2.9 %gather_fusion.2 = bf16[4,128,1024]{2,1,0:T(8,128)(2,1)} fusion(bf16[4,128,1024]{2,1,0:T(8,128)(2,1)} %pad_maximum_fusion, s32[1024]{0:T(1024)S(1)} %pad_clamp_fusion), kind=kCustom, calls=%fused_computation.2 | custom fusion | bytes 2097168 | tf_op jit(solution)/shard_map/jit(_take)/gather | solution.py:41
  109.1 1.6 select_reduce_fusion
  111.1 1.6 broadcast_in_dim.134
  112.7 4.3 %all-to-all-start.2 = ((bf16[8,128,1024]{2,1,0:T(8,128)(2,1)}), bf16[8,128,1024]{2,1,0:T(8,128)(2,1)}, u32[]{:S(2)}, u32[]{:S(2)}) async-start(bf16[8,128,1024]{2,1,0:T(8,128)(2,1)} %broadcast_in_dim.134), calls=%async_computation.2 | async-start | bytes 4194304 | tf_op jit(solution)/shard_map/all_to_all | solution.py:132
  117.1 2.8 %fusion.23 = (bf16[8,1,128,4,128]{2,4,3,1,0:T(8,128)(2,1)S(1)}, bf16[8,1,128,4,128]{2,4,3,1,0:T(8,128)(2,1)}) fusion(bf16[8,2,128,4,128]{2,4,3,1,0:T(8,128)(2,1)} %all-to-all-done.1), kind=kLoop, calls=%fused_computation.88 | loop fusion | bytes 4194304 | tf_op jit(solution)/shard_map/slice | solution.py:142
  119.9 37.8 %all-reduce.2.cloned.1.call-done = bf16[1024,1024]{1,0:T(8,128)(2,1)} async-done(((bf16[1024,1024]{1,0:T(8,128)(2,1)}), bf16[1024,1024]{1,0:T(8,128)(2,1)}) %all-reduce.2.cloned.1.call-update) | async-done | bytes 2097168 | tf_op jit(solution)/shard_map/psum | solution.py:116
  157.7 3.7 %fusion = f32[1024]{0:T(1024)S(1)} fusion(bf16[1024,1024]{1,0:T(8,128)(2,1)} %all-reduce.2.cloned.1.call-done, f32[1024,1024]{1,0:T(8,128)} %all-gather.2.cloned.1.call-done, f32[1024]{0:T(1024)S(1)} %add_rsqrt_fusion), kind=kLoop, calls=%fused_computation.7 | loop fusion | flops 4193280 | bytes 6299648 | tf_op jit(solution)/shard_map/reduce_sum | solution.py:19
  161.7 0.7 copy-done.2
  162.4 0.8 fusion.2
  163.2 3.2 %fusion.4 = f32[4,128,1024,1]{2,1,3,0:T(8,128)S(1)} fusion(bf16[8,128,1024]{2,1,0:T(8,128)(2,1)} %all-to-all-done.2, bf16[8,1,128,4,128]{2,4,3,1,0:T(8,128)(2,1)} %get-tuple-element.32), kind=kOutput, calls=%fused_computation.16 | convolution fusion | flops 1073741824 | bytes 5242880 | tf_op jit(solution)/shard_map/mqgr,mqe->gre/dot_general | solution.py:140
  166.4 2.9 %select_convert_fusion = (bf16[4,128,1024]{2,1,0:T(8,128)(2,1)}, f32[4,128,1024]{2,1,0:T(8,128)}) fusion(pred[4]{0:T(512)(128)(4,1)S(1)} %iota_compare_fusion.1, bf16[8,128,1024,1]{2,1,0,3:T(8,128)(2,1)S(1)} %bitcast.116, bf16[8,1,128,4,128]{2,4,3,1,0:T(8,128)(2,1)S(1)} %get-tuple-element.31, f32[4,128,1024,1]{2,1,3,0:T(8,128)S(1)} %fusion.4), kind=kOutput, calls=%fused_computation.18 | convolution fusion | flops 1074790400 | bytes 8388612 | tf_op jit(solution)/shard_map/mqgr,mqe->gre/dot_general | solution.py:142
  169.3 7.2 %convolution_convert_fusion.1 = bf16[128,4096]{1,0:T(8,128)(2,1)} fusion(bf16[128,1024]{1,0:T(8,128)(2,1)S(1)} %multiply_convert_fusion.2, bf16[4096,1024]{1,0:T(8,128)(2,1)} %param.11), kind=kOutput, calls=%fused_computation.6 | convolution fusion | flops 1074266112 | bytes 9699328 | tf_op jit(solution)/shard_map/qe,de->qd/dot_general | solution.py:126
  176.6 7.2 %convolution_convert_fusion = bf16[128,4096]{1,0:T(8,128)(2,1)} fusion(bf16[4096,1024]{1,0:T(8,128)(2,1)} %param.11, bf16[1024,1024]{1,0:T(8,128)(2,1)S(1)} %fusion.2, s32[]{:T(128)S(6)} %select_n.153), kind=kOutput, calls=%fused_computation.5 | convolution fusion | flops 1074266112 | bytes 9699332 | tf_op jit(solution)/shard_map/qe,de->qd/dot_general | solution.py:129
  183.8 12.3 %reduce-scatter.2.cloned.1.call-done = bf16[1,128,1024]{2,1,0:T(8,128)(2,1)} async-done(((bf16[4,128,1024]{2,1,0:T(8,128)(2,1)}), bf16[1,128,1024]{2,1,0:T(8,128)(2,1)}) %reduce-scatter.2.cloned.1.call-update) | async-done | bytes 262160 | tf_op jit(solution)/shard_map/reduce_scatter | solution.py:145
  196.1 2.0 convert_add_fusion
  (64 shorter events, 3.5 us)
Async XLA Ops:
  7.2 5.9 %copy-start.9 = (s32[1,16]{1,0:T(1,128)S(1)}, s32[1,16]{1,0:T(1,128)}, u32[]{:S(2)}) copy-start(s32[1,16]{1,0:T(1,128)} %param.12) | copy-start | bytes 196
  7.2 13.0 %copy-start.5 = (bf16[128,4096]{1,0:T(8,128)(2,1)S(1)}, bf16[128,4096]{1,0:T(8,128)(2,1)}, u32[]{:S(2)}) copy-start(bf16[128,4096]{1,0:T(8,128)(2,1)} %param.9) | copy-start | bytes 3145732
  7.2 45.4 %all-gather.2.cloned.1.call-start = ((), (), s32[]{:S(2)}) async-start(), calls=%async_computation.4 | async-start | bytes 4718592 | tf_op jit(solution)/shard_map/all_gather | solution.py:62
  13.1 23.4 %collective-permute-start = (s32[16]{0:T(128)S(1)}, s32[16]{0:T(128)S(1)}, u32[]{:S(2)}, u32[]{:S(2)}) collective-permute-start(s32[16]{0:T(128)S(1)} %bitcast.128), channel_id=1, source_target_pairs={{0,8},{8,16},{16,24},{24,0},{1,9},{9,17},{17,25},{25,1},{2,10},{10... | collective-permute-start | bytes 200 | tf_op jit(solution)/shard_map/ppermute | solution.py:28
  16.2 20.3 %collective-permute-start.1 = (s32[16]{0:T(128)S(1)}, s32[16]{0:T(128)S(1)}, u32[]{:S(2)}, u32[]{:S(2)}) collective-permute-start(s32[16]{0:T(128)S(1)} %bitcast.129), channel_id=1, source_target_pairs={{0,16},{8,24},{16,0},{24,8},{1,17},{9,25},{17,1},{25,9},{2,18},{10... | collective-permute-start | bytes 200 | tf_op jit(solution)/shard_map/ppermute | solution.py:28
  18.8 17.7 %collective-permute-start.2 = (s32[16]{0:T(128)S(1)}, s32[16]{0:T(128)S(1)}, u32[]{:S(2)}, u32[]{:S(2)}) collective-permute-start(s32[16]{0:T(128)S(1)} %bitcast.130), channel_id=1, source_target_pairs={{0,24},{8,0},{16,8},{24,16},{1,25},{9,1},{17,9},{25,17},{2,26},{10... | collective-permute-start | bytes 200 | tf_op jit(solution)/shard_map/ppermute | solution.py:28
  25.1 1.2 copy-start.3
  26.4 5.1 %copy-start.6 = (bf16[128,4096]{1,0:T(8,128)(2,1)S(1)}, bf16[128,4096]{1,0:T(8,128)(2,1)}, u32[]{:S(2)}) copy-start(bf16[128,4096]{1,0:T(8,128)(2,1)} %param.10) | copy-start | bytes 3145732
  26.4 28.7 %all-to-all-start = ((bf16[4,128,1024]{2,1,0:T(8,128)(2,1)}), bf16[4,128,1024]{2,1,0:T(8,128)(2,1)S(1)}, u32[]{:S(2)}, u32[]{:S(2)}) async-start(bf16[4,128,1024]{2,1,0:T(8,128)(2,1)} %broadcast_in_dim.126), calls=%async_computation | async-start | bytes 2097152 | tf_op jit(solution)/shard_map/all_to_all | solution.py:71
  31.4 1.3 copy-start.7
  55.1 56.0 %all-to-all-start.1 = ((bf16[8,2,128,4,128]{2,4,3,1,0:T(8,128)(2,1)}), bf16[8,2,128,4,128]{2,4,3,1,0:T(8,128)(2,1)}, u32[]{:S(2)}, u32[]{:S(2)}) async-start(bf16[8,2,128,4,128]{2,4,3,1,0:T(8,128)(2,1)} %copy.25), calls=%async_computation.1 | async-start | bytes 4194304 | tf_op jit(solution)/shard_map/all_to_all | solution.py:60
  59.5 98.2 %all-reduce.2.cloned.1.call-start = ((), (), s32[]{:S(2)}) async-start(), calls=%async_computation.5 | async-start | bytes 4194304 | tf_op jit(solution)/shard_map/psum | solution.py:116
  63.2 0.7 copy-start.8
  63.8 4.6 %collective-permute-start.4 = (f32[3,4,128]{2,1,0:T(4,128)S(1)}, f32[3,4,128]{2,1,0:T(4,128)S(1)}, u32[]{:S(2)}, u32[]{:S(2)}) collective-permute-start(f32[3,4,128]{2,1,0:T(4,128)S(1)} %get-tuple-element.38), channel_id=1, source_target_pairs={{0,16},{8,24},{16,0},{24,8},{1,17},{9,25},{17,1},{25,9},{2,18},{10... | collective-permute-start | bytes 18440 | tf_op jit(solution)/shard_map/ppermute | solution.py:28
  66.3 3.6 %collective-permute-start.5 = (f32[3,4,128]{2,1,0:T(4,128)S(1)}, f32[3,4,128]{2,1,0:T(4,128)S(1)}, u32[]{:S(2)}, u32[]{:S(2)}) collective-permute-start(f32[3,4,128]{2,1,0:T(4,128)S(1)} %get-tuple-element.38), channel_id=1, source_target_pairs={{0,24},{8,0},{16,8},{24,16},{1,25},{9,1},{17,9},{25,17},{2,26},{10... | collective-permute-start | bytes 18440 | tf_op jit(solution)/shard_map/ppermute | solution.py:28
  67.7 5.4 %collective-permute-start.3 = (f32[3,4,128]{2,1,0:T(4,128)S(1)}, f32[3,4,128]{2,1,0:T(4,128)S(1)}, u32[]{:S(2)}, u32[]{:S(2)}) collective-permute-start(f32[3,4,128]{2,1,0:T(4,128)S(1)} %get-tuple-element.38), channel_id=1, source_target_pairs={{0,8},{8,16},{16,24},{24,0},{1,9},{9,17},{17,25},{25,1},{2,10},{10... | collective-permute-start | bytes 18440 | tf_op jit(solution)/shard_map/ppermute | solution.py:28
  75.5 2.2 %copy-start.1 = (bf16[4,128,1024]{2,1,0:T(8,128)(2,1)}, bf16[4,128,1024]{2,1,0:T(8,128)(2,1)S(1)}, u32[]{:S(2)}) copy-start(bf16[4,128,1024]{2,1,0:T(8,128)(2,1)S(1)} %multiply_convert_fusion.1) | copy-start | bytes 3145732
  84.9 11.3 %collective-permute-start.6 = (bf16[128,1024]{1,0:T(8,128)(2,1)}, bf16[128,1024]{1,0:T(8,128)(2,1)S(1)}, u32[]{:S(2)}, u32[]{:S(2)}) collective-permute-start(bf16[128,1024]{1,0:T(8,128)(2,1)} %get-tuple-element.36), channel_id=1, source_target_pairs={{0,8},{8,16},{16,24},{24,0},{1,9},{9,17},{17,25},{25,1},{2,10},{10... | collective-permute-start | bytes 786440 | tf_op jit(solution)/shard_map/ppermute | solution.py:39
  84.9 20.2 %collective-permute-start.7 = (bf16[128,1024]{1,0:T(8,128)(2,1)}, bf16[128,1024]{1,0:T(8,128)(2,1)S(1)}, u32[]{:S(2)}, u32[]{:S(2)}) collective-permute-start(bf16[128,1024]{1,0:T(8,128)(2,1)} %get-tuple-element.35), channel_id=1, source_target_pairs={{0,16},{8,24},{16,0},{24,8},{1,17},{9,25},{17,1},{25,9},{2,18},{10... | collective-permute-start | bytes 786440 | tf_op jit(solution)/shard_map/ppermute | solution.py:39
  85.4 19.6 %collective-permute-start.8 = (bf16[128,1024]{1,0:T(8,128)(2,1)}, bf16[128,1024]{1,0:T(8,128)(2,1)S(1)}, u32[]{:S(2)}, u32[]{:S(2)}) collective-permute-start(bf16[128,1024]{1,0:T(8,128)(2,1)} %get-tuple-element.34), channel_id=1, source_target_pairs={{0,24},{8,0},{16,8},{24,16},{1,25},{9,1},{17,9},{25,17},{2,26},{10... | collective-permute-start | bytes 786440 | tf_op jit(solution)/shard_map/ppermute | solution.py:39
  106.2 4.5 %copy-start.4 = (f32[128,1024]{1,0:T(8,128)S(1)}, f32[128,1024]{1,0:T(8,128)}, u32[]{:S(2)}) copy-start(f32[128,1024]{1,0:T(8,128)} %copy-done.3) | copy-start | bytes 1572868
  112.7 50.5 %all-to-all-start.2 = ((bf16[8,128,1024]{2,1,0:T(8,128)(2,1)}), bf16[8,128,1024]{2,1,0:T(8,128)(2,1)}, u32[]{:S(2)}, u32[]{:S(2)}) async-start(bf16[8,128,1024]{2,1,0:T(8,128)(2,1)} %broadcast_in_dim.134), calls=%async_computation.2 | async-start | bytes 4194304 | tf_op jit(solution)/shard_map/all_to_all | solution.py:132
  117.1 79.1 %reduce-scatter.2.cloned.1.call-start = ((), (), s32[]{:S(2)}) async-start(), calls=%async_computation.6 | async-start | bytes 1310720 | tf_op jit(solution)/shard_map/reduce_scatter | solution.py:145
  157.7 4.0 %copy-start = (f32[1024,1024]{1,0:T(8,128)S(1)}, f32[1024,1024]{1,0:T(8,128)}, u32[]{:S(2)}) copy-start(f32[1024,1024]{1,0:T(8,128)} %all-gather.2.cloned.1.call-done) | copy-start | bytes 12582916
  157.7 4.7 %copy-start.2 = (bf16[1024,1024]{1,0:T(8,128)(2,1)S(1)}, bf16[1024,1024]{1,0:T(8,128)(2,1)}, u32[]{:S(2)}) copy-start(bf16[1024,1024]{1,0:T(8,128)(2,1)} %all-reduce.2.cloned.1.call-done) | copy-start | bytes 6291460
Sparse Core Ops, SparseCore 0:
  13.2 39.2 all-gather.1
  88.8 68.7 all-reduce.1
  169.5 26.6 reduce-scatter.1
where the time goes:
time: 205 us
  waiting for transfers between devices  86.3 us (42%)
  matrix products  43.5 us (21%)
  starting transfers between devices  27.8 us (14%)
  other arithmetic  17.9 us (9%)
  local copies, waits for them, and re-layouts  15 us (7%)
  between operations  14 us (7%)
    psum x1, waiting for transfers between devices, body(): code_delta = lax.psum(code_sum, 'member').astype(jnp.float32)  37.8 us
    ppermute x3, waiting for transfers between devices, exchange(): lax.ppermute(sent, axis, [(i, (i + s) % size) for i in range(size)])  16.4 us
    all_gather x1, waiting for transfers between devices, body(): lax.all_gather(jnp.dot(code_feat, projection, preferred_element_type=jnp....  15 us
    reduce_scatter x1, waiting for transfers between devices, body(): lax.psum_scatter(sent_proj, 'group', scatter_dimension=0, tiled=True)  12.3 us
    ppermute x6, starting transfers between devices, shift_all(): lax.ppermute(x, axis, [(i, (i + s) % size) for i in range(size)])  11.5 us
    dot_general x1, matrix products, body(): jnp.einsum('qe,de->qd', dz_query, projection, preferred_element_type=jnp....  7.24 us
    dot_general x1, matrix products, body(): jnp.einsum('qe,de->qd', dz_code, projection, preferred_element_type=jnp.f...  7.24 us
    dot_general x1, matrix products, body(): jnp.dot(code_feat, projection, preferred_element_type=jnp.float32)  5.85 us
  transfers between devices with their start and end apart: 15, of which 8 were waited for; matrix products, arithmetic and copies ran while one was open for 30% of the time, Pallas kernels for 0%

commit v1 on v0

--- a/solution.py
+++ b/solution.py
@@ -59,11 +59,24 @@
     feats = jnp.transpose(feats, (3, 0, 1, 2, 4))
     feat_cols = lax.all_to_all(feats, "member", split_axis=0, concat_axis=0, tiled=True)
     q_unit, q_inv, q_emb = embed(query_feat, projection)
-    code_values = lax.all_gather(
-        jnp.dot(code_feat, projection, preferred_element_type=jnp.float32),
-        "member",
-        axis=0,
-        tiled=True,
+
+    def _return_all_scales(inputs):
+        ax_name = "member"
+        left_arr = jax.lax.axis_size(ax_name)
+        local_out = jax.lax.axis_index(ax_name)
+        moved, val2, view_out = (left_arr, local_out, inputs.shape[0])
+        newest, tile_out = (inputs, 1)
+        while tile_out < moved:
+            w2 = range(moved)
+            arr_out = map(lambda no: (no, (no - tile_out) % moved), w2)
+            now = list(arr_out)
+            kept_arr = jax.lax.ppermute(newest, axis_name=ax_name, perm=now)
+            newest = jnp.concatenate([newest, kept_arr], 0)
+            tile_out = 2 * tile_out
+        return jnp.roll(newest, val2 * view_out, 0)
+
+    code_values = _return_all_scales(
+        jnp.dot(code_feat, projection, preferred_element_type=jnp.float32)
     )
     c_inv = lax.rsqrt(jnp.sum(code_values * code_values, axis=1) + epsilon)
     c_unit = code_values * c_inv[:, None]

time: 205 us -> 308 us (1.50)
  waiting for transfers between devices: 86.3 us -> 166 us
  local copies, waits for them, and re-layouts: 15 us -> 25.5 us
  other arithmetic: 17.9 us -> 24 us
  starting transfers between devices: 27.8 us -> 31.6 us
    ppermute x0 -> x3, waiting for transfers between devices: none -> 54.9 us  [_return_all_scales(): kept_arr = jax.lax.ppermute(newest, axis_name=ax_name, perm=now)]
    psum x1, waiting for transfers between devices: 37.8 us -> 77.6 us  [body(): code_delta = lax.psum(code_sum, 'member').astype(jnp.float32)]
    all_gather x1 -> x0, waiting for transfers between devices: 15 us -> none  [body(): lax.all_gather(jnp.dot(code_feat, projection, preferred_element_type=jnp....]
    unnamed x22 -> x26, local copies, waits for them, and re-layouts: 3.84 us -> 12.9 us
    ppermute x0 -> x3, starting transfers between devices: none -> 4.4 us  [_return_all_scales(): kept_arr = jax.lax.ppermute(newest, axis_name=ax_name, perm=now)]
    dot_general x4, matrix products: 4.6 us -> 8.38 us  [body(): term = jnp.dot(grad[g].T, q_all[g], preferred_element_type=jnp.float32)]
    dot_general x1, matrix products: 4.98 us -> 1.42 us  [embed(): values = jnp.dot(features, projection, preferred_element_type=jnp.float32)]
    convert_element_type x2, other arithmetic: 0.98 us -> 4.22 us  [norm_back(): (inverse[:, None] * (upstream - unit_vec * inner_prod)).astype(jnp.bfloat16)]
  transfers between devices with their start and end apart: 15 -> 17, of which waited for: 8 -> 9; matrix products, arithmetic and copies ran while one was open for 30% -> 25% of each run, Pallas kernels for 0% -> 0%
where the time goes in v1:
time: 308 us; the launch traced here: 307 us
  waiting for transfers between devices  166 us (54%)
  matrix products  45.1 us (15%)
  starting transfers between devices  31.6 us (10%)
  local copies, waits for them, and re-layouts  25.5 us (8%)
  other arithmetic  24 us (8%)
  between operations  14.3 us (5%)
    psum x1, waiting for transfers between devices, body(): code_delta = lax.psum(code_sum, 'member').astype(jnp.float32)  77.6 us
    ppermute x3, waiting for transfers between devices, _return_all_scales(): kept_arr = jax.lax.ppermute(newest, axis_name=ax_name, perm=now)  54.9 us
    ppermute x3, waiting for transfers between devices, exchange(): lax.ppermute(sent, axis, [(i, (i + s) % size) for i in range(size)])  16.2 us
    unnamed x26, local copies, waits for them, and re-layouts  12.9 us
    reduce_scatter x1, waiting for transfers between devices, body(): lax.psum_scatter(sent_proj, 'group', scatter_dimension=0, tiled=True)  12 us
    ppermute x6, starting transfers between devices, shift_all(): lax.ppermute(x, axis, [(i, (i + s) % size) for i in range(size)])  10.2 us
    dot_general x4, matrix products, body(): term = jnp.dot(grad[g].T, q_all[g], preferred_element_type=jnp.float32)  8.38 us
    dot_general x1, matrix products, body(): jnp.einsum('qe,de->qd', dz_code, projection, preferred_element_type=jnp.f...  7.24 us
  transfers between devices with their start and end apart: 17, of which 9 were waited for; matrix products, arithmetic and copies ran while one was open for 25% of the time, Pallas kernels for 0%

profile of v1, /device:TPU:0, one launch (start us, length us, event | category | flops | bytes accessed | tf_op | source)
XLA Modules:
  0.0 306.9 jit_solution(4779380462408494592)
XLA Ops:
  7.2 5.9 %constant_dynamic-update-slice_fusion.7 = (f32[2048,1024]{1,0:T(8,128)}, f32[128,1024]{1,0:T(8,128)S(1)}) fusion(bf16[128,4096]{1,0:T(8,128)(2,1)} %param.10, bf16[4096,1024]{1,0:T(8,128)(2,1)} %param.11), kind=kOutput, calls=%fused_computation.63 | convolution fusion | flops 1073741824 | bytes 10485760 | tf_op jit(solution)/shard_map/dot_general | solution.py:79
  13.1 3.4 %collective-permute-start.3 = (f32[128,1024]{1,0:T(8,128)S(1)}, f32[128,1024]{1,0:T(8,128)S(1)}, u32[]{:S(2)}, u32[]{:S(2)}) collective-permute-start(f32[128,1024]{1,0:T(8,128)S(1)} %get-tuple-element.42), channel_id=1, source_target_pairs={{0,7},{1,0},{2,1},{3,2},{4,3},{5,4},{6,5},{7,6},{8,15},{9,8},{10,9... | collective-permute-start | bytes 1572872 | tf_op jit(solution)/shard_map/ppermute | solution.py:73
  16.5 6.7 %collective-permute-done.3 = f32[128,1024]{1,0:T(8,128)S(1)} collective-permute-done((f32[128,1024]{1,0:T(8,128)S(1)}, f32[128,1024]{1,0:T(8,128)S(1)}, u32[]{:S(2)}, u32[]{:S(2)}) %collective-permute-start.3) | collective-permute-done | bytes 524320 | tf_op jit(solution)/shard_map/ppermute | solution.py:73
  23.8 1.6 collective-permute-start
  25.4 2.6 collective-permute-start.1
  28.0 1.3 collective-permute-start.2
  29.4 1.4 multiply_reduce_fusion.2
  30.8 18.0 %collective-permute-done.4 = f32[256,1024]{1,0:T(8,128)S(1)} collective-permute-done((f32[256,1024]{1,0:T(8,128)S(1)}, f32[256,1024]{1,0:T(8,128)S(1)}, u32[]{:S(2)}, u32[]{:S(2)}) %collective-permute-start.4) | collective-permute-done | bytes 1048608 | tf_op jit(solution)/shard_map/ppermute | solution.py:73
  48.9 1.5 pad_maximum_fusion
  52.0 4.9 %all-to-all-start = ((bf16[4,128,1024]{2,1,0:T(8,128)(2,1)}), bf16[4,128,1024]{2,1,0:T(8,128)(2,1)}, u32[]{:S(2)}, u32[]{:S(2)}) async-start(bf16[4,128,1024]{2,1,0:T(8,128)(2,1)} %broadcast_in_dim.126), calls=%async_computation | async-start | bytes 2097152 | tf_op jit(solution)/shard_map/all_to_all | solution.py:84
  56.9 2.3 copy.23
  59.2 1.3 copy.24
  60.5 1.7 maximum_bitcast_fusion
  62.2 1.5 copy.25
  67.7 30.2 %collective-permute-done.5 = f32[512,1024]{1,0:T(8,128)} collective-permute-done((f32[512,1024]{1,0:T(8,128)}, f32[512,1024]{1,0:T(8,128)}, u32[]{:S(2)}, u32[]{:S(2)}) %collective-permute-start.5) | collective-permute-done | bytes 2097184 | tf_op jit(solution)/shard_map/ppermute | solution.py:73
  97.9 3.1 %constant_dynamic-update-slice_fusion.4 = f32[2048,1024]{1,0:T(8,128)} fusion(f32[2048,1024]{1,0:T(8,128)} %constant_dynamic-update-slice_fusion.5, f32[512,1024]{1,0:T(8,128)} %collective-permute-done.5), kind=kLoop, calls=%fused_computation.60 | loop fusion | bytes 4194304
  103.8 3.2 %constant_dynamic-update-slice_fusion = f32[2048,1024]{1,0:T(8,128)} fusion(f32[2048,1024]{1,0:T(8,128)} %constant_dynamic-update-slice_fusion.1, f32[512,1024]{1,0:T(8,128)} %collective-permute-done.5), kind=kLoop, calls=%fused_computation.56 | loop fusion | bytes 4194304 | tf_op jit(solution)/shard_map/jit(_roll_dynamic)/concatenate | solution.py:76
  107.0 2.5 multiply_reduce_fusion
  109.6 3.6 %all-to-all-start.1 = ((bf16[8,2,128,4,128]{2,4,3,1,0:T(8,128)(2,1)}), bf16[8,2,128,4,128]{2,4,3,1,0:T(8,128)(2,1)S(1)}, u32[]{:S(2)}, u32[]{:S(2)}) async-start(bf16[8,2,128,4,128]{2,4,3,1,0:T(8,128)(2,1)} %copy.25), calls=%async_computation.1 | async-start | bytes 4194304 | tf_op jit(solution)/shard_map/all_to_all | solution.py:60
  113.2 4.0 %fusion.27 = (f32[4,128]{1,0:T(4,128)S(1)}, f32[4,128,1024]{2,1,0:T(8,128)S(1)}) fusion(bf16[4,128,1024]{2,1,0:T(8,128)(2,1)} %all-to-all-done, f32[2048,1024]{1,0:T(8,128)} %constant_dynamic-update-slice_fusion, s32[]{:T(128)S(6)} %select_n.150, f32[1024]{0:T(1024)S(1)} %add_rsqrt_fusion, pred[4,1024]{1,0:T(4,128)(4,1)S(1)} %broadcast_in_dim.124), kind=kOutput, calls=%fused_computation.102 | convolution fusion | flops 1077411328 | bytes 7350276 | tf_op jit(solution)/shard_map/gqe,ke->gqk/dot_general | solution.py:99
  117.2 1.3 copy-done.3
  119.1 2.7 collective-permute-start.7
  121.7 1.3 collective-permute-start.8
  123.7 1.6 collective-permute-done.8
  125.3 3.1 %collective-permute-done.6 = f32[3,4,128]{2,1,0:T(4,128)S(1)} collective-permute-done((f32[3,4,128]{2,1,0:T(4,128)S(1)}, f32[3,4,128]{2,1,0:T(4,128)S(1)}, u32[]{:S(2)}, u32[]{:S(2)}) %collective-permute-start.6) | collective-permute-done | bytes 6176 | tf_op jit(solution)/shard_map/ppermute | solution.py:28
  129.2 2.2 multiply_convert_fusion
  131.4 1.7 fusion.12
  133.1 1.7 fusion.13
  134.8 1.7 fusion.11
  136.5 3.4 %add_convert_fusion = bf16[1024,1024]{1,0:T(8,128)(2,1)} fusion(f32[1024,1024]{1,0:T(8,128)S(1)} %fusion.11, f32[1024,1024]{1,0:T(8,128)S(1)} %fusion.12, f32[1024,1024]{1,0:T(8,128)S(1)} %fusion.13, pred[]{:T(512)S(6)} %eq.78, pred[]{:T(512)S(6)} %eq.77, pred[]{:T(512)S(6)} %eq.76, pred[]{:T(512)S(6)} %eq.75, bf16[4,128,1024]{2,1,0:T(8,128)(2,1)} %all-to-all-done, ...), kind=kOutput, calls=%fused_computation.10 | convolution fusion | flops 285212672 | bytes 15204356 | tf_op jit(solution)/shard_map/dot_general | solution.py:124
  139.8 4.8 %fusion.28 = (bf16[4,128,1024]{2,1,0:T(8,128)(2,1)S(1)}, f32[4,128,1024]{2,1,0:T(8,128)}) fusion(bf16[4,128,1024]{2,1,0:T(8,128)(2,1)S(1)} %multiply_convert_fusion, f32[2048,1024]{1,0:T(8,128)} %constant_dynamic-update-slice_fusion, s32[]{:T(128)S(6)} %select_n.150, f32[1024]{0:T(1024)S(1)} %add_rsqrt_fusion), kind=kOutput, calls=%fused_computation.103 | convolution fusion | flops 1076363264 | bytes 8392708 | tf_op jit(solution)/shard_map/gqk,ke->gqe/dot_general | solution.py:130
  145.4 3.3 %collective-permute-start.11 = (bf16[128,1024]{1,0:T(8,128)(2,1)S(1)}, bf16[128,1024]{1,0:T(8,128)(2,1)S(1)}, u32[]{:S(2)}, u32[]{:S(2)}) collective-permute-start(bf16[128,1024]{1,0:T(8,128)(2,1)S(1)} %get-tuple-element.34), channel_id=1, source_target_pairs={{0,24},{8,0},{16,8},{24,16},{1,25},{9,1},{17,9},{25,17},{2,26},{10... | collective-permute-start | bytes 786440 | tf_op jit(solution)/shard_map/ppermute | solution.py:39
  148.6 7.2 %collective-permute-done.9 = bf16[128,1024]{1,0:T(8,128)(2,1)S(1)} collective-permute-done((bf16[128,1024]{1,0:T(8,128)(2,1)S(1)}, bf16[128,1024]{1,0:T(8,128)(2,1)S(1)}, u32[]{:S(2)}, u32[]{:S(2)}) %collective-permute-start.9) | collective-permute-done | bytes 262176 | tf_op jit(solution)/shard_map/ppermute | solution.py:39
  155.9 9.0 %collective-permute-done.10 = bf16[128,1024]{1,0:T(8,128)(2,1)S(1)} collective-permute-done((bf16[128,1024]{1,0:T(8,128)(2,1)S(1)}, bf16[128,1024]{1,0:T(8,128)(2,1)S(1)}, u32[]{:S(2)}, u32[]{:S(2)}) %collective-permute-start.10) | collective-permute-done | bytes 262176 | tf_op jit(solution)/shard_map/ppermute | solution.py:39
  166.0 2.8 gather_fusion.2
  168.8 1.6 select_reduce_fusion
  170.4 1.2 multiply_reduce_fusion.1
  172.9 1.6 broadcast_in_dim.134
  174.5 4.4 %all-to-all-start.2 = ((bf16[8,128,1024]{2,1,0:T(8,128)(2,1)}), bf16[8,128,1024]{2,1,0:T(8,128)(2,1)}, u32[]{:S(2)}, u32[]{:S(2)}) async-start(bf16[8,128,1024]{2,1,0:T(8,128)(2,1)} %broadcast_in_dim.134), calls=%async_computation.2 | async-start | bytes 4194304 | tf_op jit(solution)/shard_map/all_to_all | solution.py:145
  181.1 77.6 %all-reduce.2.cloned.1.call-done = bf16[1024,1024]{1,0:T(8,128)(2,1)} async-done(((bf16[1024,1024]{1,0:T(8,128)(2,1)}), bf16[1024,1024]{1,0:T(8,128)(2,1)}) %all-reduce.2.cloned.1.call-update) | async-done | bytes 2097168 | tf_op jit(solution)/shard_map/psum | solution.py:129
  258.7 3.7 %fusion = f32[1024]{0:T(1024)S(1)} fusion(bf16[1024,1024]{1,0:T(8,128)(2,1)} %all-reduce.2.cloned.1.call-done, f32[2048,1024]{1,0:T(8,128)} %constant_dynamic-update-slice_fusion, s32[]{:T(128)S(6)} %select_n.150, f32[1024]{0:T(1024)S(1)} %add_rsqrt_fusion), kind=kLoop, calls=%fused_computation.7 | loop fusion | flops 4193280 | bytes 6299652 | tf_op jit(solution)/shard_map/reduce_sum | solution.py:19
  262.4 3.0 fusion.2
  265.4 3.2 %fusion.5 = f32[4,128,1024,1]{2,1,3,0:T(8,128)S(1)} fusion(bf16[8,128,1024]{2,1,0:T(8,128)(2,1)} %all-to-all-done.2, bf16[8,1,128,4,128]{2,4,3,1,0:T(8,128)(2,1)} %get-tuple-element.32), kind=kOutput, calls=%fused_computation.18 | convolution fusion | flops 1073741824 | bytes 5242880 | tf_op jit(solution)/shard_map/mqgr,mqe->gre/dot_general | solution.py:153
  268.6 2.9 select_convert_fusion
  271.5 7.2 %convolution_convert_fusion.1 = bf16[128,4096]{1,0:T(8,128)(2,1)} fusion(bf16[128,1024]{1,0:T(8,128)(2,1)S(1)} %multiply_convert_fusion.1, bf16[4096,1024]{1,0:T(8,128)(2,1)} %param.11), kind=kOutput, calls=%fused_computation.6 | convolution fusion | flops 1074266112 | bytes 9699328 | tf_op jit(solution)/shard_map/qe,de->qd/dot_general | solution.py:139
  278.8 7.2 %convolution_convert_fusion = bf16[128,4096]{1,0:T(8,128)(2,1)} fusion(bf16[4096,1024]{1,0:T(8,128)(2,1)} %param.11, bf16[1024,1024]{1,0:T(8,128)(2,1)S(1)} %fusion.2, s32[]{:T(128)S(6)} %select_n.167), kind=kOutput, calls=%fused_computation.5 | convolution fusion | flops 1074266112 | bytes 9699332 | tf_op jit(solution)/shard_map/qe,de->qd/dot_general | solution.py:142
  286.0 12.0 %reduce-scatter.2.cloned.1.call-done = bf16[1,128,1024]{2,1,0:T(8,128)(2,1)} async-done(((bf16[4,128,1024]{2,1,0:T(8,128)(2,1)}), bf16[1,128,1024]{2,1,0:T(8,128)(2,1)}) %reduce-scatter.2.cloned.1.call-update) | async-done | bytes 262160 | tf_op jit(solution)/shard_map/reduce_scatter | solution.py:158
  298.1 2.0 convert_add_fusion
  (74 shorter events, 16.2 us)
Async XLA Ops:
  7.2 22.2 %copy-start = (bf16[4096,1024]{1,0:T(8,128)(2,1)S(1)}, bf16[4096,1024]{1,0:T(8,128)(2,1)}, u32[]{:S(2)}) copy-start(bf16[4096,1024]{1,0:T(8,128)(2,1)} %param.11) | copy-start | bytes 25165828
  7.2 16.7 %copy-start.8 = (s32[1,16]{1,0:T(1,128)S(1)}, s32[1,16]{1,0:T(1,128)}, u32[]{:S(2)}) copy-start(s32[1,16]{1,0:T(1,128)} %param.12) | copy-start | bytes 196
  7.2 22.2 %copy-start.6 = (bf16[128,4096]{1,0:T(8,128)(2,1)S(1)}, bf16[128,4096]{1,0:T(8,128)(2,1)}, u32[]{:S(2)}) copy-start(bf16[128,4096]{1,0:T(8,128)(2,1)} %param.9) | copy-start | bytes 3145732
  13.1 10.1 %collective-permute-start.3 = (f32[128,1024]{1,0:T(8,128)S(1)}, f32[128,1024]{1,0:T(8,128)S(1)}, u32[]{:S(2)}, u32[]{:S(2)}) collective-permute-start(f32[128,1024]{1,0:T(8,128)S(1)} %get-tuple-element.42), channel_id=1, source_target_pairs={{0,7},{1,0},{2,1},{3,2},{4,3},{5,4},{6,5},{7,6},{8,15},{9,8},{10,9... | collective-permute-start | bytes 1572872 | tf_op jit(solution)/shard_map/ppermute | solution.py:73
  23.2 25.6 %collective-permute-start.4 = (f32[256,1024]{1,0:T(8,128)S(1)}, f32[256,1024]{1,0:T(8,128)S(1)}, u32[]{:S(2)}, u32[]{:S(2)}) collective-permute-start(f32[256,1024]{1,0:T(8,128)S(1)} %pad_maximum_fusion.1), channel_id=1, source_target_pairs={{0,6},{1,7},{2,0},{3,1},{4,2},{5,3},{6,4},{7,5},{8,14},{9,15},{10,... | collective-permute-start | bytes 3145736 | tf_op jit(solution)/shard_map/ppermute | solution.py:73
  23.8 40.9 %collective-permute-start = (s32[16]{0:T(128)S(1)}, s32[16]{0:T(128)S(1)}, u32[]{:S(2)}, u32[]{:S(2)}) collective-permute-start(s32[16]{0:T(128)S(1)} %bitcast.128), channel_id=1, source_target_pairs={{0,8},{8,16},{16,24},{24,0},{1,9},{9,17},{17,25},{25,1},{2,10},{10... | collective-permute-start | bytes 200 | tf_op jit(solution)/shard_map/ppermute | solution.py:28
  25.4 39.3 %collective-permute-start.1 = (s32[16]{0:T(128)S(1)}, s32[16]{0:T(128)S(1)}, u32[]{:S(2)}, u32[]{:S(2)}) collective-permute-start(s32[16]{0:T(128)S(1)} %bitcast.129), channel_id=1, source_target_pairs={{0,16},{8,24},{16,0},{24,8},{1,17},{9,25},{17,1},{25,9},{2,18},{10... | collective-permute-start | bytes 200 | tf_op jit(solution)/shard_map/ppermute | solution.py:28
  28.0 36.7 %collective-permute-start.2 = (s32[16]{0:T(128)S(1)}, s32[16]{0:T(128)S(1)}, u32[]{:S(2)}, u32[]{:S(2)}) collective-permute-start(s32[16]{0:T(128)S(1)} %bitcast.130), channel_id=1, source_target_pairs={{0,24},{8,0},{16,8},{24,16},{1,25},{9,1},{17,9},{25,17},{2,26},{10... | collective-permute-start | bytes 200 | tf_op jit(solution)/shard_map/ppermute | solution.py:28
  30.8 20.0 %copy-start.4 = (f32[128,1024]{1,0:T(8,128)}, f32[128,1024]{1,0:T(8,128)S(1)}, u32[]{:S(2)}) copy-start(f32[128,1024]{1,0:T(8,128)S(1)} %get-tuple-element.40) | copy-start | bytes 1572868
  50.4 8.8 %copy-start.1 = (bf16[128,4096]{1,0:T(8,128)(2,1)S(1)}, bf16[128,4096]{1,0:T(8,128)(2,1)}, u32[]{:S(2)}) copy-start(bf16[128,4096]{1,0:T(8,128)(2,1)} %param.10) | copy-start | bytes 3145732
  50.4 47.5 %collective-permute-start.5 = (f32[512,1024]{1,0:T(8,128)}, f32[512,1024]{1,0:T(8,128)}, u32[]{:S(2)}, u32[]{:S(2)}) collective-permute-start(f32[512,1024]{1,0:T(8,128)} %pad_maximum_fusion), channel_id=1, source_target_pairs={{0,4},{1,5},{2,6},{3,7},{4,0},{5,1},{6,2},{7,3},{8,12},{9,13},{10,... | collective-permute-start | bytes 6291464 | tf_op jit(solution)/shard_map/ppermute | solution.py:73
  52.0 57.6 %all-to-all-start = ((bf16[4,128,1024]{2,1,0:T(8,128)(2,1)}), bf16[4,128,1024]{2,1,0:T(8,128)(2,1)}, u32[]{:S(2)}, u32[]{:S(2)}) async-start(bf16[4,128,1024]{2,1,0:T(8,128)(2,1)} %broadcast_in_dim.126), calls=%async_computation | async-start | bytes 2097152 | tf_op jit(solution)/shard_map/all_to_all | solution.py:84
  109.6 63.3 %all-to-all-start.1 = ((bf16[8,2,128,4,128]{2,4,3,1,0:T(8,128)(2,1)}), bf16[8,2,128,4,128]{2,4,3,1,0:T(8,128)(2,1)S(1)}, u32[]{:S(2)}, u32[]{:S(2)}) async-start(bf16[8,2,128,4,128]{2,4,3,1,0:T(8,128)(2,1)} %copy.25), calls=%async_computation.1 | async-start | bytes 4194304 | tf_op jit(solution)/shard_map/all_to_all | solution.py:60
  113.2 5.8 %copy-start.7 = (f32[128]{0:T(128)S(1)}, f32[128]{0:T(128)}, u32[]{:S(2)}) copy-start(f32[128]{0:T(128)} %param.13) | copy-start | bytes 1540
  117.2 1.3 copy-start.3
  119.1 4.7 %collective-permute-start.7 = (f32[3,4,128]{2,1,0:T(4,128)S(1)}, f32[3,4,128]{2,1,0:T(4,128)S(1)}, u32[]{:S(2)}, u32[]{:S(2)}) collective-permute-start(f32[3,4,128]{2,1,0:T(4,128)S(1)} %get-tuple-element.38), channel_id=1, source_target_pairs={{0,16},{8,24},{16,0},{24,8},{1,17},{9,25},{17,1},{25,9},{2,18},{10... | collective-permute-start | bytes 18440 | tf_op jit(solution)/shard_map/ppermute | solution.py:28
  121.7 3.6 %collective-permute-start.8 = (f32[3,4,128]{2,1,0:T(4,128)S(1)}, f32[3,4,128]{2,1,0:T(4,128)S(1)}, u32[]{:S(2)}, u32[]{:S(2)}) collective-permute-start(f32[3,4,128]{2,1,0:T(4,128)S(1)} %get-tuple-element.38), channel_id=1, source_target_pairs={{0,24},{8,0},{16,8},{24,16},{1,25},{9,1},{17,9},{25,17},{2,26},{10... | collective-permute-start | bytes 18440 | tf_op jit(solution)/shard_map/ppermute | solution.py:28
  123.1 5.4 %collective-permute-start.6 = (f32[3,4,128]{2,1,0:T(4,128)S(1)}, f32[3,4,128]{2,1,0:T(4,128)S(1)}, u32[]{:S(2)}, u32[]{:S(2)}) collective-permute-start(f32[3,4,128]{2,1,0:T(4,128)S(1)} %get-tuple-element.38), channel_id=1, source_target_pairs={{0,8},{8,16},{16,24},{24,0},{1,9},{9,17},{17,25},{25,1},{2,10},{10... | collective-permute-start | bytes 18440 | tf_op jit(solution)/shard_map/ppermute | solution.py:28
  144.7 25.8 %copy-start.5 = (f32[128,1024]{1,0:T(8,128)S(1)}, f32[128,1024]{1,0:T(8,128)}, u32[]{:S(2)}) copy-start(f32[128,1024]{1,0:T(8,128)} %copy-done.4) | copy-start | bytes 1572868
  144.8 11.1 %collective-permute-start.9 = (bf16[128,1024]{1,0:T(8,128)(2,1)S(1)}, bf16[128,1024]{1,0:T(8,128)(2,1)S(1)}, u32[]{:S(2)}, u32[]{:S(2)}) collective-permute-start(bf16[128,1024]{1,0:T(8,128)(2,1)S(1)} %get-tuple-element.36), channel_id=1, source_target_pairs={{0,8},{8,16},{16,24},{24,0},{1,9},{9,17},{17,25},{25,1},{2,10},{10... | collective-permute-start | bytes 786440 | tf_op jit(solution)/shard_map/ppermute | solution.py:39
  144.8 20.0 %collective-permute-start.10 = (bf16[128,1024]{1,0:T(8,128)(2,1)S(1)}, bf16[128,1024]{1,0:T(8,128)(2,1)S(1)}, u32[]{:S(2)}, u32[]{:S(2)}) collective-permute-start(bf16[128,1024]{1,0:T(8,128)(2,1)S(1)} %get-tuple-element.35), channel_id=1, source_target_pairs={{0,16},{8,24},{16,0},{24,8},{1,17},{9,25},{17,1},{25,9},{2,18},{10... | collective-permute-start | bytes 786440 | tf_op jit(solution)/shard_map/ppermute | solution.py:39
  145.4 19.5 %collective-permute-start.11 = (bf16[128,1024]{1,0:T(8,128)(2,1)S(1)}, bf16[128,1024]{1,0:T(8,128)(2,1)S(1)}, u32[]{:S(2)}, u32[]{:S(2)}) collective-permute-start(bf16[128,1024]{1,0:T(8,128)(2,1)S(1)} %get-tuple-element.34), channel_id=1, source_target_pairs={{0,24},{8,0},{16,8},{24,16},{1,25},{9,1},{17,9},{25,17},{2,26},{10... | collective-permute-start | bytes 786440 | tf_op jit(solution)/shard_map/ppermute | solution.py:39
  174.5 90.9 %all-to-all-start.2 = ((bf16[8,128,1024]{2,1,0:T(8,128)(2,1)}), bf16[8,128,1024]{2,1,0:T(8,128)(2,1)}, u32[]{:S(2)}, u32[]{:S(2)}) async-start(bf16[8,128,1024]{2,1,0:T(8,128)(2,1)} %broadcast_in_dim.134), calls=%async_computation.2 | async-start | bytes 4194304 | tf_op jit(solution)/shard_map/all_to_all | solution.py:145
  178.9 79.8 %all-reduce.2.cloned.1.call-start = ((), (), s32[]{:S(2)}) async-start(), calls=%async_computation.4 | async-start | bytes 4194304 | tf_op jit(solution)/shard_map/psum | solution.py:129
  179.6 118.4 %reduce-scatter.2.cloned.1.call-start = ((), (), s32[]{:S(2)}) async-start(), calls=%async_computation.5 | async-start | bytes 1310720 | tf_op jit(solution)/shard_map/reduce_scatter | solution.py:158
  258.7 3.7 %copy-start.2 = (bf16[1024,1024]{1,0:T(8,128)(2,1)S(1)}, bf16[1024,1024]{1,0:T(8,128)(2,1)}, u32[]{:S(2)}) copy-start(bf16[1024,1024]{1,0:T(8,128)(2,1)} %all-reduce.2.cloned.1.call-done) | copy-start | bytes 6291460
Sparse Core Ops, SparseCore 0:
  182.9 75.6 all-reduce.1
  271.7 26.3 reduce-scatter.1
